TPU v7x, 256 devices: a whole 4x4x8 slice. The times are simulated.
256 devices in a mesh: row: 8 (over y_hi, x), col: 32 (over y_lo, z, core).
Axes of the slice: x: 4, y: 4 (y_hi: 2, y_lo: 2; y = y_hi * 2 + y_lo), z: 8, core: 2. Of those that a mesh axis runs over, the one named last changes fastest.
Arguments:
- left_image: bfloat16 [64, 16384, 128], P('row', 'col'), may hold values from -9 to 9
- right_image: bfloat16 [64, 16384, 128], P('row', 'col'), may hold values from -9 to 9
- conv_weight: bfloat16 [3, 3, 128, 256], replicated, may hold values from -0.1875 to 0.1875
Outputs:
- disparity: float32 [32, 8192], P('row', 'col')
- entropy: float32 [32, 8192], P('row', 'col')
All inputs are finite; a program needn't handle non-finite values.
Results may differ from a plain program's by a relative error of at most 0.0057.
Values may be sent and summed in bfloat16 or wider, within the bound.
No kernel may reach another device: no remote copies, remote signals or barrier semaphores. Data moves between devices by JAX's collectives and lax.ppermute only.
A program may use at most 64 MiB of HBM per device.

v0:
```python
import jax
import jax.numpy as jnp
from jax import lax
from jax.sharding import PartitionSpec as P

NEG_FILL = -1e30


def from_behind(array, axis, by):
    count = lax.axis_size(axis)
    pairs = [(i, i + by) for i in range(count) if 0 <= i + by < count]
    return lax.ppermute(array, axis, pairs)


def conv_taps(padded, weights, row_count, col_count):
    total = jnp.zeros((row_count * col_count, weights.shape[-1]), jnp.float32)
    for a in range(3):
        for b in range(3):
            window = padded[a : a + 2 * row_count - 1 : 2, b : b + 2 * col_count - 1 : 2, :]
            total = total + jnp.dot(
                window.reshape(row_count * col_count, -1),
                weights[a, b],
                preferred_element_type=jnp.float32,
            )
    return total.astype(jnp.bfloat16).reshape(row_count, col_count, -1)


def empty_state(row_count, col_count):
    zeros = jnp.zeros((row_count, col_count), jnp.float32)
    return (jnp.full((row_count, col_count), NEG_FILL, jnp.float32), zeros, zeros, zeros)


def absorb(state, query, panel_keys, offset):
    peak, mass, moment, spread = state
    scores = jnp.einsum(
        "rif,rjf->rij", query, panel_keys, preferred_element_type=jnp.float32
    ) * query.shape[-1] ** (-0.5)
    offset = jnp.asarray(offset, jnp.int32).astype(jnp.float32)
    distance = (
        offset
        + jnp.arange(query.shape[1], dtype=jnp.float32)[:, None]
        - jnp.arange(panel_keys.shape[1], dtype=jnp.float32)[None, :]
    )
    allowed = distance >= 0.0
    block_peak = jnp.max(jnp.where(allowed, scores, NEG_FILL), axis=-1)
    new_peak = jnp.maximum(peak, block_peak)
    shifted = jnp.where(allowed, scores - new_peak[:, :, None], NEG_FILL)
    weights = jnp.exp(shifted)
    settled = jnp.where(allowed, shifted, 0.0)
    factor = jnp.exp(peak - new_peak)
    mass_new = mass * factor + jnp.sum(weights, axis=-1)
    moment_new = moment * factor + jnp.sum(weights * distance, axis=-1)
    spread_new = factor * (spread + (peak - new_peak) * mass) + jnp.sum(weights * settled, axis=-1)
    return (new_peak, mass_new, moment_new, spread_new)


def finish(state, col_count):
    disparity = state[2] / state[1] / col_count
    entropy = jnp.log(state[1]) - state[3] / state[1]
    return (disparity, entropy)


def local(left_image, right_image, conv_weight):
    row_count = left_image.shape[0] // 2
    col_count = left_image.shape[1] // 2
    border = jnp.stack([left_image[:, -1:, :], right_image[:, -1:, :]])
    border = from_behind(border, "col", 1)
    left_wide = jnp.concatenate([border[0], left_image], axis=1)
    right_wide = jnp.concatenate([border[1], right_image], axis=1)
    upper = from_behind(jnp.stack([left_wide[-1:], right_wide[-1:]]), "row", 1)
    left_full = jnp.concatenate([upper[0], left_wide], axis=0)
    right_full = jnp.concatenate([upper[1], right_wide], axis=0)
    left_feat = conv_taps(left_full, conv_weight, row_count, col_count)
    right_feat = conv_taps(right_full, conv_weight, row_count, col_count)
    position = lax.axis_index("col")
    start_state = empty_state(row_count, col_count)
    piece = lax.all_gather(right_feat, "col", axis=1, tiled=True)
    width_piece = piece.shape[1]
    anchor = position * col_count

    def visit(b, running):
        portion = lax.dynamic_slice_in_dim(piece, b * col_count, col_count, 1)
        return absorb(running, left_feat, portion, anchor - b * col_count)

    final = lax.fori_loop(0, width_piece // col_count, visit, start_state)
    return finish(final, col_count)


def solution(mesh):
    in_specs = (P("row", "col", None), P("row", "col", None), P())
    out_specs = (P("row", "col"), P("row", "col"))
    return jax.shard_map(local, mesh=mesh, in_specs=in_specs, out_specs=out_specs, check_vma=False)
```

profile of v0, /device:TPU:1, one launch (start us, length us, event | category | flops | bytes accessed | tf_op | source)
XLA Modules:
  0.0 227.8 jit_solution(3837790933711198921)
XLA Ops:
  8.8 4.9 %collective-permute-start = (bf16[2,8,1,128]{3,1,2,0:T(8,128)(2,1)S(1)}, bf16[2,8,1,128]{3,1,2,0:T(8,128)(2,1)S(1)}, u32[]{:S(2)}, u32[]{:S(2)}) collective-permute-start(bf16[2,8,1,128]{3,1,2,0:T(8,128)(2,1)S(1)} %pad_maximum_fusion.3), channel_id=1, source_target_pairs={{0,1},{1,2},{2,3},{3,4},{4,5},{5,6},{6,7},{7,8},{8,9},{9,10},{10,1... | collective-permute-start | bytes 12296 | tf_op jit(solution)/shard_map/ppermute | solution.py:12
  15.6 3.8 %collective-permute-start.1 = (bf16[2,1,513,128]{3,2,1,0:T(8,128)(2,1)S(1)}, bf16[2,1,513,128]{3,2,1,0:T(8,128)(2,1)}, u32[]{:S(2)}, u32[]{:S(2)}) collective-permute-start(bf16[2,1,513,128]{3,2,1,0:T(8,128)(2,1)S(1)} %pad_maximum_fusion.2), channel_id=1, source_target_pairs={{0,32},{32,64},{64,96},{96,128},{128,160},{160,192},{192,224},{1,3... | collective-permute-start | bytes 787976 | tf_op jit(solution)/shard_map/ppermute | solution.py:12
  19.4 2.6 %slice.131 = bf16[4,256,128]{2,1,0:T(8,128)(2,1)} slice(bf16[8,512,128]{2,1,0:T(8,128)(2,1)S(1)} %copy-done), slice={[0:7:2], [1:512:2], [0:128:1]} | slice | bytes 524288 | tf_op jit(solution)/shard_map/slice | solution.py:19
  22.0 2.6 %slice.129 = bf16[4,256,128]{2,1,0:T(8,128)(2,1)} slice(bf16[8,512,128]{2,1,0:T(8,128)(2,1)S(1)} %copy-done), slice={[0:7:2], [0:511:2], [0:128:1]} | slice | bytes 524288 | tf_op jit(solution)/shard_map/slice | solution.py:19
  24.6 2.7 %slice.137 = bf16[4,256,128]{2,1,0:T(8,128)(2,1)} slice(bf16[8,512,128]{2,1,0:T(8,128)(2,1)S(1)} %copy-done), slice={[1:8:2], [1:512:2], [0:128:1]} | slice | bytes 524288 | tf_op jit(solution)/shard_map/slice | solution.py:19
  27.4 2.7 %slice.135 = bf16[4,256,128]{2,1,0:T(8,128)(2,1)} slice(bf16[8,512,128]{2,1,0:T(8,128)(2,1)S(1)} %copy-done), slice={[1:8:2], [0:511:2], [0:128:1]} | slice | bytes 524288 | tf_op jit(solution)/shard_map/slice | solution.py:19
  30.4 2.7 %slice.133 = bf16[4,256,128]{2,1,0:T(8,128)(2,1)} slice(bf16[8,513,128]{2,1,0:T(8,128)(2,1)S(1)} %pad_maximum_fusion.1), slice={[1:8:2], [0:511:2], [0:128:1]} | slice | bytes 524288 | tf_op jit(solution)/shard_map/slice | solution.py:19
  33.1 2.6 %slice.127 = bf16[4,256,128]{2,1,0:T(8,128)(2,1)} slice(bf16[8,513,128]{2,1,0:T(8,128)(2,1)S(1)} %pad_maximum_fusion.1), slice={[0:7:2], [0:511:2], [0:128:1]} | slice | bytes 524288 | tf_op jit(solution)/shard_map/slice | solution.py:19
  37.0 2.6 %slice.125 = bf16[4,256,128]{2,1,0:T(8,128)(2,1)} slice(bf16[9,513,128]{2,1,0:T(8,128)(2,1)S(1)} %maximum_maximum_fusion), slice={[0:7:2], [2:513:2], [0:128:1]} | slice | bytes 524288 | tf_op jit(solution)/shard_map/slice | solution.py:19
  40.0 2.6 %slice.121 = bf16[4,256,128]{2,1,0:T(8,128)(2,1)} slice(bf16[9,513,128]{2,1,0:T(8,128)(2,1)S(1)} %maximum_maximum_fusion), slice={[0:7:2], [0:511:2], [0:128:1]} | slice | bytes 524288 | tf_op jit(solution)/shard_map/slice | solution.py:19
  51.7 2.6 %slice.145 = bf16[4,256,128]{2,1,0:T(8,128)(2,1)} slice(bf16[8,512,128]{2,1,0:T(8,128)(2,1)S(1)} %copy-done.1), slice={[0:7:2], [1:512:2], [0:128:1]} | slice | bytes 524288 | tf_op jit(solution)/shard_map/slice | solution.py:19
  54.3 2.6 %slice.144 = bf16[4,256,128]{2,1,0:T(8,128)(2,1)} slice(bf16[8,512,128]{2,1,0:T(8,128)(2,1)S(1)} %copy-done.1), slice={[0:7:2], [0:511:2], [0:128:1]} | slice | bytes 524288 | tf_op jit(solution)/shard_map/slice | solution.py:19
  58.3 2.7 %slice.146 = bf16[4,256,128]{2,1,0:T(8,128)(2,1)} slice(bf16[8,513,128]{2,1,0:T(8,128)(2,1)S(1)} %pad_maximum_fusion), slice={[1:8:2], [0:511:2], [0:128:1]} | slice | bytes 524288 | tf_op jit(solution)/shard_map/slice | solution.py:19
  61.0 2.6 %slice.143 = bf16[4,256,128]{2,1,0:T(8,128)(2,1)} slice(bf16[8,513,128]{2,1,0:T(8,128)(2,1)S(1)} %pad_maximum_fusion), slice={[0:7:2], [0:511:2], [0:128:1]} | slice | bytes 524288 | tf_op jit(solution)/shard_map/slice | solution.py:19
  70.4 85.2 %all-gather.2.cloned.1.call-done = bf16[4,8192,256]{2,1,0:T(8,128)(2,1)} async-done(((bf16[4,256,256]{2,1,0:T(8,128)(2,1)}), bf16[4,8192,256]{2,1,0:T(8,128)(2,1)}) %all-gather.2.cloned.1.call-update) | async-done | bytes 16777232 | tf_op jit(solution)/shard_map/all_gather | solution.py:77
  155.5 64.8 %while.20 = (s32[]{:T(128)}, f32[4,256]{1,0:T(4,128)S(1)}, f32[4,256]{1,0:T(4,128)S(1)}, f32[4,256]{1,0:T(4,128)S(1)}, f32[4,256]{1,0:T(4,128)S(1)}, /*index=5*/...) while((s32[]{:T(128)}, f32[4,256]{1,0:T(4,128)S(1)}, ...), condition=%wide.region_5.6_spmd.clone, body=%wide.region_0.5_spmd.clone.sunk | while | flops 137309440 | bytes 3955922 | solution.py:85
  155.7 1.4 select_reduce_fusion.2
  157.7 1.4 select_reduce_fusion.2
  159.7 1.4 select_reduce_fusion.2
  161.8 1.4 select_reduce_fusion.2
  163.8 1.4 select_reduce_fusion.2
  165.8 1.4 select_reduce_fusion.2
  167.8 1.4 select_reduce_fusion.2
  169.9 1.4 select_reduce_fusion.2
  171.9 1.4 select_reduce_fusion.2
  173.9 1.4 select_reduce_fusion.2
  175.9 1.4 select_reduce_fusion.2
  178.0 1.4 select_reduce_fusion.2
  180.0 1.4 select_reduce_fusion.2
  182.0 1.4 select_reduce_fusion.2
  184.0 1.4 select_reduce_fusion.2
  186.1 1.4 select_reduce_fusion.2
  188.1 1.4 select_reduce_fusion.2
  190.1 1.4 select_reduce_fusion.2
  192.1 1.4 select_reduce_fusion.2
  194.2 1.4 select_reduce_fusion.2
  196.2 1.4 select_reduce_fusion.2
  198.2 1.4 select_reduce_fusion.2
  200.2 1.4 select_reduce_fusion.2
  202.3 1.4 select_reduce_fusion.2
  204.3 1.4 select_reduce_fusion.2
  206.3 1.4 select_reduce_fusion.2
  208.3 1.4 select_reduce_fusion.2
  210.4 1.4 select_reduce_fusion.2
  212.4 1.4 select_reduce_fusion.2
  214.4 1.4 select_reduce_fusion.2
  216.4 1.4 select_reduce_fusion.2
  218.5 1.4 select_reduce_fusion.2
  (300 shorter events, 40.7 us)
Async XLA Ops:
  7.2 8.3 %copy-start.1 = (bf16[8,512,128]{2,1,0:T(8,128)(2,1)S(1)}, bf16[8,512,128]{2,1,0:T(8,128)(2,1)}, u32[]{:S(2)}) copy-start(bf16[8,512,128]{2,1,0:T(8,128)(2,1)} %param.5) | copy-start | bytes 3145732
  7.2 148.4 %all-gather.2.cloned.1.call-start = ((), (), s32[]{:S(2)}) async-start(), calls=%async_computation | async-start | bytes 17301504 | tf_op jit(solution)/shard_map/all_gather | solution.py:77
  8.8 5.7 %collective-permute-start = (bf16[2,8,1,128]{3,1,2,0:T(8,128)(2,1)S(1)}, bf16[2,8,1,128]{3,1,2,0:T(8,128)(2,1)S(1)}, u32[]{:S(2)}, u32[]{:S(2)}) collective-permute-start(bf16[2,8,1,128]{3,1,2,0:T(8,128)(2,1)S(1)} %pad_maximum_fusion.3), channel_id=1, source_target_pairs={{0,1},{1,2},{2,3},{3,4},{4,5},{5,6},{6,7},{7,8},{8,9},{9,10},{10,1... | collective-permute-start | bytes 12296 | tf_op jit(solution)/shard_map/ppermute | solution.py:12
  14.5 5.0 %copy-start = (bf16[8,512,128]{2,1,0:T(8,128)(2,1)S(1)}, bf16[8,512,128]{2,1,0:T(8,128)(2,1)}, u32[]{:S(2)}) copy-start(bf16[8,512,128]{2,1,0:T(8,128)(2,1)} %param.6) | copy-start | bytes 3145732
  15.6 20.1 %collective-permute-start.1 = (bf16[2,1,513,128]{3,2,1,0:T(8,128)(2,1)S(1)}, bf16[2,1,513,128]{3,2,1,0:T(8,128)(2,1)}, u32[]{:S(2)}, u32[]{:S(2)}) collective-permute-start(bf16[2,1,513,128]{3,2,1,0:T(8,128)(2,1)S(1)} %pad_maximum_fusion.2), channel_id=1, source_target_pairs={{0,32},{32,64},{64,96},{96,128},{128,160},{160,192},{192,224},{1,3... | collective-permute-start | bytes 787976 | tf_op jit(solution)/shard_map/ppermute | solution.py:12
  37.0 5.6 %copy-start.2 = (bf16[3,3,128,256]{3,2,1,0:T(8,128)(2,1)S(1)}, bf16[3,3,128,256]{3,2,1,0:T(8,128)(2,1)}, u32[]{:S(2)}) copy-start(bf16[3,3,128,256]{3,2,1,0:T(8,128)(2,1)} %param.7) | copy-start | bytes 1769476
  43.9 1.0 copy-start.12
  44.8 0.9 copy-start.10
  45.8 0.9 copy-start.8
  46.7 0.9 copy-start.5
  47.7 0.9 copy-start.6
  48.6 0.9 copy-start.3
  49.6 0.9 copy-start.13
  65.7 1.0 copy-start.11
  66.6 1.0 copy-start.7
  67.6 0.9 copy-start.4
  68.6 0.9 copy-start.9
Sparse Core Ops, SparseCore 0:
  51.8 103.7 all-gather.1
where the time goes:
time: 230 us; the launch traced here: 228 us
  waiting for transfers between devices  85.9 us (37%)
  matrix products  51.6 us (22%)
  local copies, waits for them, and re-layouts  44.5 us (19%)
  other arithmetic  20.5 us (9%)
  between operations  14.3 us (6%)
  starting transfers between devices  8.8 us (4%)
    all_gather x1, waiting for transfers between devices, local(): piece = lax.all_gather(right_feat, 'col', axis=1, tiled=True)  85.2 us
    dot_general x32, matrix products, absorb(): jnp.einsum('rif,rjf->rij', query, panel_keys, preferred_element_type=jnp....  44.9 us
    slice x18, local copies, waits for them, and re-layouts, conv_taps(): window = padded[a:a + 2 * row_count - 1:2, b:b + 2 * col_count - 1:2, :]  34.4 us
    reduce_sum x32, other arithmetic, absorb(): jnp.sum(weights * settled, axis=-1)  12.7 us
    ppermute x2, starting transfers between devices, from_behind(): return lax.ppermute(array, axis, pairs)  8.76 us
    unnamed x28, local copies, waits for them, and re-layouts  7.4 us
    dot_general x18, matrix products, conv_taps(): jnp.dot(window.reshape(row_count * col_count, -1), weights[a, b], preferr...  6.72 us
  transfers between devices with their start and end apart: 3, of which 2 were waited for; matrix products, arithmetic and copies ran while one was open for 14% of the time, Pallas kernels for 0%

commit v1 on v0

v1 whole, which is shorter than its diff:
```python
import numpy as np
import jax
import jax.numpy as jnp
from jax import lax
from jax.experimental import pallas as pl
from jax.experimental.pallas import tpu as pltpu
from jax.sharding import Mesh, PartitionSpec as P

NEG_FILL = -1e30
COL = ("colc", "core")


def from_behind(array, axis, by):
    count = lax.axis_size(axis)
    pairs = [(i, i + by) for i in range(count) if 0 <= i + by < count]
    return lax.ppermute(array, axis, pairs)


def encode(full, weights):
    out = lax.conv_general_dilated(
        full[None],
        weights,
        window_strides=(2, 2),
        padding="VALID",
        dimension_numbers=("NHWC", "HWIO", "NHWC"),
        preferred_element_type=jnp.float32,
    )
    return out[0].astype(jnp.bfloat16)


def corr_kernel(qb_ref, q_ref, k_ref, disp_ref, ent_ref, *, blk, dev_cols):
    qb0 = qb_ref[0]
    width = q_ref.shape[1]
    q = q_ref[0]
    scale = q.shape[-1] ** (-0.5)
    qpos = (qb0 * blk).astype(jnp.float32) + lax.broadcasted_iota(jnp.int32, (1, width), 1).astype(jnp.float32)
    jcol = lax.broadcasted_iota(jnp.int32, (blk, 1), 0).astype(jnp.float32)

    def step(kb, state, masked):
        peak, mass, moment, spread = state
        start = pl.multiple_of(kb * blk, blk)
        keys = k_ref[0, pl.ds(start, blk), :]
        scores = lax.dot_general(
            keys, q, (((1,), (1,)), ((), ())), preferred_element_type=jnp.float32
        ) * scale
        base = qpos - (kb * blk).astype(jnp.float32)
        if masked:
            allowed = (base - jcol) >= 0.0
            scores = jnp.where(allowed, scores, NEG_FILL)
        new_peak = jnp.maximum(peak, jnp.max(scores, axis=0, keepdims=True))
        shifted = scores - new_peak
        if masked:
            shifted = jnp.where(allowed, shifted, NEG_FILL)
        weights = jnp.exp(shifted)
        if masked:
            settled = jnp.where(allowed, shifted, 0.0)
        else:
            settled = shifted
        factor = jnp.exp(peak - new_peak)
        total = jnp.sum(weights, axis=0, keepdims=True)
        mass_new = mass * factor + total
        moment_new = moment * factor + (
            base * total - jnp.sum(weights * jcol, axis=0, keepdims=True)
        )
        spread_new = factor * (spread + (peak - new_peak) * mass) + jnp.sum(
            weights * settled, axis=0, keepdims=True
        )
        return (new_peak, mass_new, moment_new, spread_new)

    zeros = jnp.zeros((1, width), jnp.float32)
    state = (jnp.full((1, width), NEG_FILL, jnp.float32), zeros, zeros, zeros)
    state = lax.fori_loop(0, qb0, lambda kb, s: step(kb, s, False), state)
    for extra in range(width // blk):
        state = step(qb0 + extra, state, True)
    peak, mass, moment, spread = state
    disp_ref[0] = moment / mass / dev_cols
    ent_ref[0] = jnp.log(mass) - spread / mass


def correlate(qb0, queries, keys, dev_cols):
    rows, width, feat = queries.shape
    total_cols = keys.shape[1]
    blk = dev_cols
    kernel = lambda *refs: corr_kernel(*refs, blk=blk, dev_cols=dev_cols)
    out_shape = jax.ShapeDtypeStruct((rows, 1, width), jnp.float32)
    disp, ent = pl.pallas_call(
        kernel,
        out_shape=(out_shape, out_shape),
        grid_spec=pltpu.PrefetchScalarGridSpec(
            num_scalar_prefetch=1,
            grid=(rows,),
            in_specs=[
                pl.BlockSpec((1, width, feat), lambda r, s: (r, 0, 0)),
                pl.BlockSpec((1, total_cols, feat), lambda r, s: (r, 0, 0)),
            ],
            out_specs=[
                pl.BlockSpec((1, 1, width), lambda r, s: (r, 0, 0)),
                pl.BlockSpec((1, 1, width), lambda r, s: (r, 0, 0)),
            ],
        ),
        compiler_params=pltpu.CompilerParams(dimension_semantics=("arbitrary",)),
    )(qb0, queries, keys)
    return disp.reshape(rows, width), ent.reshape(rows, width)


def local(left_image, right_image, conv_weight):
    col_count = left_image.shape[1] // 2
    border = jnp.stack([left_image[:, -1:, :], right_image[:, -1:, :]])
    border = from_behind(border, COL, 1)
    left_wide = jnp.concatenate([border[0], left_image], axis=1)
    right_wide = jnp.concatenate([border[1], right_image], axis=1)
    upper = from_behind(jnp.stack([left_wide[-1:], right_wide[-1:]]), "row", 1)
    left_full = jnp.concatenate([upper[0], left_wide], axis=0)
    right_full = jnp.concatenate([upper[1], right_wide], axis=0)
    right_feat = encode(right_full, conv_weight)
    right_half = lax.all_to_all(right_feat, "core", 0, 1, tiled=True)
    keys = lax.all_gather(right_half, "colc", axis=1, tiled=True)
    left_feat = encode(left_full, conv_weight)
    queries = lax.all_to_all(left_feat, "core", 0, 1, tiled=True)
    pair = lax.axis_index("colc")
    qb0 = jnp.reshape(pair * 2, (1,)).astype(jnp.int32)
    disp, ent = correlate(qb0, queries, keys, col_count)
    disp = lax.all_to_all(disp, "core", 1, 0, tiled=True)
    ent = lax.all_to_all(ent, "core", 1, 0, tiled=True)
    return disp, ent


def solution(mesh):
    rows, cols = mesh.devices.shape
    split = Mesh(np.asarray(mesh.devices).reshape(rows, cols // 2, 2), ("row", "colc", "core"))
    in_specs = (P("row", COL, None), P("row", COL, None), P())
    out_specs = (P("row", COL), P("row", COL))
    return jax.shard_map(local, mesh=split, in_specs=in_specs, out_specs=out_specs, check_vma=False)
```

time: 230 us -> 190 us (0.83)
  the two profiles are of different devices: /device:TPU:1 before, /device:TPU:233 now
where the time goes in v1:
time: 190 us; the launch traced here: 189 us
  waiting for transfers between devices  93.1 us (49%)
  Pallas kernels  33.1 us (17%)
  blocking collectives  19 us (10%)
  matrix products  16.8 us (9%)
  between operations  14.2 us (7%)
  local copies, waits for them, and re-layouts  4.77 us (3%)
  starting transfers between devices  4.46 us (2%)
  other arithmetic  3.9 us (2%)
    all_gather x1, waiting for transfers between devices, local(): keys = lax.all_gather(right_half, 'colc', axis=1, tiled=True)  87.8 us
    pallas_call x1, Pallas kernels, correlate(): pl.pallas_call(kernel, out_shape=(out_shape, out_shape), grid_spec=pltpu....  33.1 us
    conv_general_dilated x2, matrix products, encode(): lax.conv_general_dilated(full[None], weights, window_strides=(2, 2), padd...  16.8 us
    all_to_all x1, blocking collectives, local(): right_half = lax.all_to_all(right_feat, 'core', 0, 1, tiled=True)  7.16 us
    ppermute x2, waiting for transfers between devices, from_behind(): return lax.ppermute(array, axis, pairs)  5.26 us
    ppermute x2, starting transfers between devices, from_behind(): return lax.ppermute(array, axis, pairs)  4.42 us
    all_to_all x1, blocking collectives, local(): queries = lax.all_to_all(left_feat, 'core', 0, 1, tiled=True)  4.15 us
    all_to_all x1, blocking collectives, local(): disp = lax.all_to_all(disp, 'core', 1, 0, tiled=True)  4.03 us
  transfers between devices with their start and end apart: 3, of which 3 were waited for; matrix products, arithmetic and copies ran while one was open for 5% of the time, Pallas kernels for 0%

profile of v1, /device:TPU:233, one launch (start us, length us, event | category | flops | bytes accessed | tf_op | source)
XLA Modules:
  0.0 189.3 jit_solution(9292447040112973120)
XLA Ops:
  7.2 0.0 copy-start
  7.2 0.0 copy-start.1
  7.2 0.0 all-gather.2.cloned.1.call-start
  7.2 0.8 slice.25
  8.1 0.7 slice.24
  8.8 1.3 collective-permute-start
  10.1 1.9 %collective-permute-done = bf16[2,8,1,128]{3,1,2,0:T(8,128)(2,1)S(1)} collective-permute-done((bf16[2,8,1,128]{3,1,2,0:T(8,128)(2,1)S(1)}, bf16[2,8,1,128]{3,1,2,0:T(8,128)(2,1)S(1)}, u32[]{:S(2)}, u32[]{:S(2)}) %collective-permute-start) | collective-permute-done | bytes 4128 | tf_op jit(solution)/shard_map/ppermute | solution.py:16
  12.1 0.9 fusion.10
  13.0 0.9 fusion.11
  14.0 3.1 %collective-permute-start.1 = (bf16[2,1,513,128]{3,2,1,0:T(8,128)(2,1)S(1)}, bf16[2,1,513,128]{3,2,1,0:T(8,128)(2,1)S(1)}, u32[]{:S(2)}, u32[]{:S(2)}) collective-permute-start(bf16[2,1,513,128]{3,2,1,0:T(8,128)(2,1)S(1)} %pad_maximum_fusion), channel_id=1, source_target_pairs={{0,32},{32,64},{64,96},{96,128},{128,160},{160,192},{192,224},{1,3... | collective-permute-start | bytes 787976 | tf_op jit(solution)/shard_map/ppermute | solution.py:16
  17.1 3.3 %collective-permute-done.1 = bf16[2,1,513,128]{3,2,1,0:T(8,128)(2,1)S(1)} collective-permute-done((bf16[2,1,513,128]{3,2,1,0:T(8,128)(2,1)S(1)}, bf16[2,1,513,128]{3,2,1,0:T(8,128)(2,1)S(1)}, u32[]{:S(2)}, u32[]{:S(2)}) %collective-permute-start.1) | collective-permute-done | bytes 262688 | tf_op jit(solution)/shard_map/ppermute | solution.py:16
  20.5 0.0 copy-done.1
  20.5 0.3 maximum_bitcast_fusion.1
  20.8 0.0 copy-done
  20.8 8.4 %fusion.7 = bf16[1,4,256,256]{3,0,2,1:T(2,128)(2,1)S(1)} fusion(bf16[3,3,128,256]{3,2,1,0:T(8,128)(2,1)S(1)} %copy-done, bf16[1,9,513,128]{3,2,1,0:T(8,128)(2,1)S(1)} %maximum_bitcast_fusion.1), kind=kOutput, calls=%fused_computation.5 | convolution fusion | flops 604241920 | bytes 2296064 | tf_op jit(solution)/shard_map/conv_general_dilated | solution.py:20
  29.2 0.0 copy-start.2
  29.3 0.1 copy.57
  29.4 7.2 %all_to_all.74 = bf16[4,256,256]{2,1,0:T(8,128)(2,1)S(1)} all-to-all(bf16[4,256,256]{2,1,0:T(8,128)(2,1)S(1)} %bitcast.42), channel_id=1, replica_groups=mesh['row'=8,'colc'=16,'core'=2] {'core'}, dimensions={0} | all-to-all | bytes 1048576 | tf_op jit(solution)/shard_map/all_to_all | solution.py:116
  36.5 0.9 copy.38
  37.4 0.0 all-gather.2.cloned.1.call-update
  37.4 0.0 copy-done.2
  37.4 0.3 maximum_bitcast_fusion
  37.7 8.4 %fusion.4 = bf16[1,4,256,256]{3,0,2,1:T(2,128)(2,1)S(1)} fusion(bf16[3,3,128,256]{3,2,1,0:T(8,128)(2,1)S(1)} %copy-done, bf16[1,9,513,128]{3,2,1,0:T(8,128)(2,1)S(1)} %maximum_bitcast_fusion), kind=kOutput, calls=%fused_computation.4 | convolution fusion | flops 604241920 | bytes 2296064 | tf_op jit(solution)/shard_map/conv_general_dilated | solution.py:20
  46.1 0.1 copy.58
  46.2 4.2 %all_to_all.75 = bf16[4,256,256]{2,1,0:T(8,128)(2,1)S(1)} all-to-all(bf16[4,256,256]{2,1,0:T(8,128)(2,1)S(1)} %bitcast.43), channel_id=1, replica_groups=mesh['row'=8,'colc'=16,'core'=2] {'core'}, dimensions={0} | all-to-all | bytes 1048576 | tf_op jit(solution)/shard_map/all_to_all | solution.py:119
  50.4 0.9 copy.36
  51.3 87.8 %all-gather.2.cloned.1.call-done.refs_2_ = bf16[2,8192,256]{2,1,0:T(8,128)(2,1)} async-done(((bf16[2,512,256]{2,1,0:T(8,128)(2,1)}), bf16[2,8192,256]{2,1,0:T(8,128)(2,1)}) %all-gather.2.cloned.1.call-update) | async-done | bytes 8388624 | tf_op jit(solution)/shard_map/all_gather | solution.py:117
  139.1 33.1 %shard_map.50 = (f32[2,1,512]{2,1,0:T(1,128)}, f32[2,1,512]{2,1,0:T(1,128)}) custom-call(s32[1]{0:T(128)} %bitcast.refs_0_, bf16[2,512,256]{2,1,0:T(8,128)(2,1)} %bitcast.41, bf16[2,8192,256]{2,1,0:T(8,128)(2,1)} %all-gather.2.cloned.1.call-done.refs_2_), custom_call_target="tpu_custom_call" | custom-call | tf_op jit(solution)/shard_map/pallas_call | solution.py:86
  172.2 0.7 reduce
  172.9 4.0 %all_to_all.76 = f32[2,2,256]{2,0,1:T(2,128)S(1)} all-to-all(f32[2,2,256]{2,0,1:T(2,128)S(1)} %bitcast.48), channel_id=1, replica_groups=mesh['row'=8,'colc'=16,'core'=2] {'core'}, dimensions={1} | all-to-all | bytes 8192 | tf_op jit(solution)/shard_map/all_to_all | solution.py:123
  176.9 0.6 all_to_all.65
  177.5 0.7 reduce.1
  178.2 3.7 %all_to_all.77 = f32[2,2,256]{2,0,1:T(2,128)S(1)} all-to-all(f32[2,2,256]{2,0,1:T(2,128)S(1)} %bitcast.47), channel_id=1, replica_groups=mesh['row'=8,'colc'=16,'core'=2] {'core'}, dimensions={1} | all-to-all | bytes 8192 | tf_op jit(solution)/shard_map/all_to_all | solution.py:124
  181.9 0.6 all_to_all.69
  (7 shorter events, 0.1 us)
Async XLA Ops:
  7.2 13.6 %copy-start = (bf16[3,3,128,256]{3,2,1,0:T(8,128)(2,1)S(1)}, bf16[3,3,128,256]{3,2,1,0:T(8,128)(2,1)}, u32[]{:S(2)}) copy-start(bf16[3,3,128,256]{3,2,1,0:T(8,128)(2,1)} %param.5) | copy-start | bytes 1769476
  7.2 13.3 %copy-start.1 = (bf16[8,512,128]{2,1,0:T(8,128)(2,1)S(1)}, bf16[8,512,128]{2,1,0:T(8,128)(2,1)}, u32[]{:S(2)}) copy-start(bf16[8,512,128]{2,1,0:T(8,128)(2,1)} %param.4) | copy-start | bytes 3145732
  7.2 131.9 %all-gather.2.cloned.1.call-start = ((), (), s32[]{:S(2)}) async-start(), calls=%async_computation.4 | async-start | bytes 8912896 | tf_op jit(solution)/shard_map/all_gather | solution.py:117
  8.8 3.2 %collective-permute-start = (bf16[2,8,1,128]{3,1,2,0:T(8,128)(2,1)S(1)}, bf16[2,8,1,128]{3,1,2,0:T(8,128)(2,1)S(1)}, u32[]{:S(2)}, u32[]{:S(2)}) collective-permute-start(bf16[2,8,1,128]{3,1,2,0:T(8,128)(2,1)S(1)} %pad_maximum_fusion.3), channel_id=1, source_target_pairs={{0,1},{1,2},{2,3},{3,4},{4,5},{5,6},{6,7},{7,8},{8,9},{9,10},{10,1... | collective-permute-start | bytes 12296 | tf_op jit(solution)/shard_map/ppermute | solution.py:16
  14.0 6.5 %collective-permute-start.1 = (bf16[2,1,513,128]{3,2,1,0:T(8,128)(2,1)S(1)}, bf16[2,1,513,128]{3,2,1,0:T(8,128)(2,1)S(1)}, u32[]{:S(2)}, u32[]{:S(2)}) collective-permute-start(bf16[2,1,513,128]{3,2,1,0:T(8,128)(2,1)S(1)} %pad_maximum_fusion), channel_id=1, source_target_pairs={{0,32},{32,64},{64,96},{96,128},{128,160},{160,192},{192,224},{1,3... | collective-permute-start | bytes 787976 | tf_op jit(solution)/shard_map/ppermute | solution.py:16
  29.2 8.2 %copy-start.2 = (bf16[8,512,128]{2,1,0:T(8,128)(2,1)S(1)}, bf16[8,512,128]{2,1,0:T(8,128)(2,1)}, u32[]{:S(2)}) copy-start(bf16[8,512,128]{2,1,0:T(8,128)(2,1)} %param.3) | copy-start | bytes 3145732
Sparse Core Ops, SparseCore 0:
  37.5 101.5 all-gather.1

commit v2 on v1

--- a/solution.py
+++ b/solution.py
@@ -114,15 +114,22 @@
     right_full = jnp.concatenate([upper[1], right_wide], axis=0)
     right_feat = encode(right_full, conv_weight)
     right_half = lax.all_to_all(right_feat, "core", 0, 1, tiled=True)
-    keys = lax.all_gather(right_half, "colc", axis=1, tiled=True)
+    keys = [
+        lax.all_gather(right_half[r : r + 1], "colc", axis=1, tiled=True)
+        for r in range(right_half.shape[0])
+    ]
     left_feat = encode(left_full, conv_weight)
     queries = lax.all_to_all(left_feat, "core", 0, 1, tiled=True)
     pair = lax.axis_index("colc")
     qb0 = jnp.reshape(pair * 2, (1,)).astype(jnp.int32)
-    disp, ent = correlate(qb0, queries, keys, col_count)
-    disp = lax.all_to_all(disp, "core", 1, 0, tiled=True)
-    ent = lax.all_to_all(ent, "core", 1, 0, tiled=True)
-    return disp, ent
+    parts = [
+        correlate(qb0, queries[r : r + 1], keys[r], col_count) for r in range(len(keys))
+    ]
+    both = jnp.stack(
+        [jnp.concatenate([p[0] for p in parts]), jnp.concatenate([p[1] for p in parts])]
+    )
+    both = lax.all_to_all(both, "core", 2, 1, tiled=True)
+    return both[0], both[1]
 
 
 def solution(mesh):

time: 190 us -> 227 us (1.19)
  waiting for transfers between devices: 93.1 us -> 118 us
  blocking collectives: 19 us -> 24.7 us
  Pallas kernels: 33.1 us -> 36.1 us
  local copies, waits for them, and re-layouts: 4.77 us -> 7.72 us
    all_gather x1 -> x2, waiting for transfers between devices: 87.8 us -> 113 us  [local(): lax.all_gather(right_half[r:r + 1], 'colc', axis=1, tiled=True)]
    all_to_all x2 -> x1, blocking collectives: 7.72 us -> 13.3 us  [local(): both = lax.all_to_all(both, 'core', 2, 1, tiled=True)]
    pallas_call x1 -> x2, Pallas kernels: 33.1 us -> 36.1 us  [correlate(): pl.pallas_call(kernel, out_shape=(out_shape, out_shape), grid_spec=pltpu....]
    slice x0 -> x5, local copies, waits for them, and re-layouts: none -> 2.33 us  [the longest x1 0.88 us: local(): right_half[r:r + 1]]
  transfers between devices with their start and end apart: 3 -> 4, of which waited for: 3 -> 4; matrix products, arithmetic and copies ran while one was open for 5% -> 4% of each run, Pallas kernels for 0% -> 8%
where the time goes in v2:
time: 227 us
  waiting for transfers between devices  118 us (52%)
  Pallas kernels  36.1 us (16%)
  blocking collectives  24.7 us (11%)
  matrix products  16.8 us (7%)
  between operations  14.2 us (6%)
  local copies, waits for them, and re-layouts  7.72 us (3%)
  other arithmetic  4.53 us (2%)
  starting transfers between devices  4.5 us (2%)
    all_gather x2, waiting for transfers between devices, local(): lax.all_gather(right_half[r:r + 1], 'colc', axis=1, tiled=True)  113 us
    pallas_call x2, Pallas kernels, correlate(): pl.pallas_call(kernel, out_shape=(out_shape, out_shape), grid_spec=pltpu....  36.1 us
    conv_general_dilated x2, matrix products, encode(): lax.conv_general_dilated(full[None], weights, window_strides=(2, 2), padd...  16.8 us
    all_to_all x1, blocking collectives, local(): both = lax.all_to_all(both, 'core', 2, 1, tiled=True)  13.3 us
    all_to_all x1, blocking collectives, local(): right_half = lax.all_to_all(right_feat, 'core', 0, 1, tiled=True)  7.16 us
    ppermute x2, waiting for transfers between devices, from_behind(): return lax.ppermute(array, axis, pairs)  5.26 us
  transfers between devices with their start and end apart: 4, of which 4 were waited for; matrix products, arithmetic and copies ran while one was open for 4% of the time, Pallas kernels for 8%

profile of v2, /device:TPU:233, one launch (start us, length us, event | category | flops | bytes accessed | tf_op | source)
XLA Modules:
  0.0 227.0 jit_solution(9987964685794760084)
XLA Ops:
  7.2 0.0 copy-start
  7.2 0.0 copy-start.1
  7.2 0.0 all-gather.5.cloned.1.call-start
  7.2 0.8 slice.57
  8.1 0.7 slice.56
  8.8 1.3 collective-permute-start
  10.1 1.9 collective-permute-done
  12.1 0.9 fusion.10
  13.0 0.9 fusion.11
  14.0 3.1 %collective-permute-start.1 = (bf16[2,1,513,128]{3,2,1,0:T(8,128)(2,1)S(1)}, bf16[2,1,513,128]{3,2,1,0:T(8,128)(2,1)S(1)}, u32[]{:S(2)}, u32[]{:S(2)}) collective-permute-start(bf16[2,1,513,128]{3,2,1,0:T(8,128)(2,1)S(1)} %pad_maximum_fusion), channel_id=1, source_target_pairs={{0,32},{32,64},{64,96},{96,128},{128,160},{160,192},{192,224},{1,3... | collective-permute-start | bytes 787976 | tf_op jit(solution)/shard_map/ppermute | solution.py:16
  17.2 3.3 %collective-permute-done.1 = bf16[2,1,513,128]{3,2,1,0:T(8,128)(2,1)S(1)} collective-permute-done((bf16[2,1,513,128]{3,2,1,0:T(8,128)(2,1)S(1)}, bf16[2,1,513,128]{3,2,1,0:T(8,128)(2,1)S(1)}, u32[]{:S(2)}, u32[]{:S(2)}) %collective-permute-start.1) | collective-permute-done | bytes 262688 | tf_op jit(solution)/shard_map/ppermute | solution.py:16
  20.5 0.0 copy-done.1
  20.5 0.3 maximum_bitcast_fusion.1
  20.8 0.0 copy-done
  20.8 8.4 %fusion.7 = bf16[1,4,256,256]{3,0,2,1:T(2,128)(2,1)S(1)} fusion(bf16[3,3,128,256]{3,2,1,0:T(8,128)(2,1)S(1)} %copy-done, bf16[1,9,513,128]{3,2,1,0:T(8,128)(2,1)S(1)} %maximum_bitcast_fusion.1), kind=kOutput, calls=%fused_computation.5 | convolution fusion | flops 604241920 | bytes 2296064 | tf_op jit(solution)/shard_map/conv_general_dilated | solution.py:20
  29.3 0.0 copy-start.2
  29.3 0.1 copy.64
  29.4 7.2 %all_to_all.45 = bf16[4,256,256]{2,1,0:T(8,128)(2,1)S(1)} all-to-all(bf16[4,256,256]{2,1,0:T(8,128)(2,1)S(1)} %bitcast.54), channel_id=1, replica_groups=mesh['row'=8,'colc'=16,'core'=2] {'core'}, dimensions={0} | all-to-all | bytes 1048576 | tf_op jit(solution)/shard_map/all_to_all | solution.py:116
  36.6 0.9 fusion.13
  37.5 0.0 all-gather.5.cloned.1.call-update
  37.5 0.0 all-gather.3.cloned.1.call-start
  37.5 0.7 all-gather.3.cloned.1.call-update
  38.2 0.0 copy-done.2
  38.2 0.3 maximum_bitcast_fusion
  38.5 8.4 %fusion.4 = bf16[1,4,256,256]{3,0,2,1:T(2,128)(2,1)S(1)} fusion(bf16[3,3,128,256]{3,2,1,0:T(8,128)(2,1)S(1)} %copy-done, bf16[1,9,513,128]{3,2,1,0:T(8,128)(2,1)S(1)} %maximum_bitcast_fusion), kind=kOutput, calls=%fused_computation.4 | convolution fusion | flops 604241920 | bytes 2296064 | tf_op jit(solution)/shard_map/conv_general_dilated | solution.py:20
  47.0 0.1 copy.65
  47.1 4.2 %all_to_all.46 = bf16[4,256,256]{2,1,0:T(8,128)(2,1)S(1)} all-to-all(bf16[4,256,256]{2,1,0:T(8,128)(2,1)S(1)} %bitcast.55), channel_id=1, replica_groups=mesh['row'=8,'colc'=16,'core'=2] {'core'}, dimensions={0} | all-to-all | bytes 1048576 | tf_op jit(solution)/shard_map/all_to_all | solution.py:122
  51.3 0.8 fusion.14
  52.1 55.5 %all-gather.5.cloned.1.call-done.refs_2_ = bf16[1,8192,256]{2,1,0:T(8,128)(2,1)} async-done(((bf16[1,512,256]{2,1,0:T(8,128)(2,1)}), bf16[1,8192,256]{2,1,0:T(8,128)(2,1)}) %all-gather.5.cloned.1.call-update) | async-done | bytes 4194320 | tf_op jit(solution)/shard_map/all_gather | solution.py:118
  107.6 18.0 %shard_map.51 = (f32[1,1,512]{2,1,0:T(1,128)}, f32[1,1,512]{2,1,0:T(1,128)}) custom-call(s32[1]{0:T(128)} %bitcast.refs_0_, bf16[1,512,256]{2,1,0:T(8,128)(2,1)} %bitcast.63, bf16[1,8192,256]{2,1,0:T(8,128)(2,1)} %all-gather.5.cloned.1.call-done.refs_2_), custom_call_target="tpu_custom_call" | custom-call | tf_op jit(solution)/shard_map/pallas_call | solution.py:86
  125.6 0.0 copy-start.4
  125.6 57.0 %all-gather.3.cloned.1.call-done.refs_2_ = bf16[1,8192,256]{2,1,0:T(8,128)(2,1)} async-done(((bf16[1,512,256]{2,1,0:T(8,128)(2,1)}), bf16[1,8192,256]{2,1,0:T(8,128)(2,1)}) %all-gather.3.cloned.1.call-update) | async-done | bytes 4194320 | tf_op jit(solution)/shard_map/all_gather | solution.py:118
  182.6 18.1 %shard_map.50 = (f32[1,1,512]{2,1,0:T(1,128)}, f32[1,1,512]{2,1,0:T(1,128)}) custom-call(s32[1]{0:T(128)} %bitcast.refs_0_, bf16[1,512,256]{2,1,0:T(8,128)(2,1)} %bitcast.62, bf16[1,8192,256]{2,1,0:T(8,128)(2,1)} %all-gather.3.cloned.1.call-done.refs_2_), custom_call_target="tpu_custom_call" | custom-call | tf_op jit(solution)/shard_map/pallas_call | solution.py:86
  200.7 0.0 copy-done.4
  200.7 0.7 maximum_bitcast_fusion.3
  201.4 0.0 copy-done.3
  201.4 0.7 maximum_bitcast_fusion.2
  202.1 0.3 copy.43
  202.3 0.7 reshape.34
  203.0 13.3 %all_to_all.47 = f32[2,1,1024]{2,1,0:T(1,128)S(1)} all-to-all(f32[2,1,1024]{2,1,0:T(1,128)S(1)} %reshape.34), channel_id=1, replica_groups=mesh['row'=8,'colc'=16,'core'=2] {'core'}, dimensions={0} | all-to-all | bytes 16384 | tf_op jit(solution)/shard_map/all_to_all | solution.py:131
  216.3 0.5 broadcast
  216.8 0.7 reduce
  217.5 0.8 reshape.35
  218.3 0.4 fusion.12
  218.7 0.1 copy.44
  218.8 0.6 squeeze.24
  219.5 0.1 copy.45
  219.6 0.6 squeeze.25
  (11 shorter events, 0.2 us)
Async XLA Ops:
  7.2 13.7 %copy-start = (bf16[3,3,128,256]{3,2,1,0:T(8,128)(2,1)S(1)}, bf16[3,3,128,256]{3,2,1,0:T(8,128)(2,1)}, u32[]{:S(2)}) copy-start(bf16[3,3,128,256]{3,2,1,0:T(8,128)(2,1)} %param.5) | copy-start | bytes 1769476
  7.2 13.3 %copy-start.1 = (bf16[8,512,128]{2,1,0:T(8,128)(2,1)S(1)}, bf16[8,512,128]{2,1,0:T(8,128)(2,1)}, u32[]{:S(2)}) copy-start(bf16[8,512,128]{2,1,0:T(8,128)(2,1)} %param.4) | copy-start | bytes 3145732
  7.2 100.4 %all-gather.5.cloned.1.call-start = ((), (), s32[]{:S(2)}) async-start(), calls=%async_computation.4 | async-start | bytes 4456448 | tf_op jit(solution)/shard_map/all_gather | solution.py:118
  8.8 3.2 %collective-permute-start = (bf16[2,8,1,128]{3,1,2,0:T(8,128)(2,1)S(1)}, bf16[2,8,1,128]{3,1,2,0:T(8,128)(2,1)S(1)}, u32[]{:S(2)}, u32[]{:S(2)}) collective-permute-start(bf16[2,8,1,128]{3,1,2,0:T(8,128)(2,1)S(1)} %pad_maximum_fusion.4), channel_id=1, source_target_pairs={{0,1},{1,2},{2,3},{3,4},{4,5},{5,6},{6,7},{7,8},{8,9},{9,10},{10,1... | collective-permute-start | bytes 12296 | tf_op jit(solution)/shard_map/ppermute | solution.py:16
  14.0 6.5 %collective-permute-start.1 = (bf16[2,1,513,128]{3,2,1,0:T(8,128)(2,1)S(1)}, bf16[2,1,513,128]{3,2,1,0:T(8,128)(2,1)S(1)}, u32[]{:S(2)}, u32[]{:S(2)}) collective-permute-start(bf16[2,1,513,128]{3,2,1,0:T(8,128)(2,1)S(1)} %pad_maximum_fusion), channel_id=1, source_target_pairs={{0,32},{32,64},{64,96},{96,128},{128,160},{160,192},{192,224},{1,3... | collective-permute-start | bytes 787976 | tf_op jit(solution)/shard_map/ppermute | solution.py:16
  29.3 9.0 %copy-start.2 = (bf16[8,512,128]{2,1,0:T(8,128)(2,1)S(1)}, bf16[8,512,128]{2,1,0:T(8,128)(2,1)}, u32[]{:S(2)}) copy-start(bf16[8,512,128]{2,1,0:T(8,128)(2,1)} %param.3) | copy-start | bytes 3145732
  37.5 145.1 %all-gather.3.cloned.1.call-start = ((), (), s32[]{:S(2)}) async-start(), calls=%async_computation.3 | async-start | bytes 4456448 | tf_op jit(solution)/shard_map/all_gather | solution.py:118
  125.6 75.1 %copy-start.4 = (f32[1,1,512]{2,1,0:T(1,128)S(1)}, f32[1,1,512]{2,1,0:T(1,128)}, u32[]{:S(2)}) copy-start(f32[1,1,512]{2,1,0:T(1,128)} %get-tuple-element.9) | copy-start | bytes 6148
  125.6 75.8 %copy-start.3 = (f32[1,1,512]{2,1,0:T(1,128)S(1)}, f32[1,1,512]{2,1,0:T(1,128)}, u32[]{:S(2)}) copy-start(f32[1,1,512]{2,1,0:T(1,128)} %get-tuple-element.7) | copy-start | bytes 6148
Sparse Core Ops, SparseCore 0:
  37.6 69.9 all-gather.4
  109.4 73.1 all-gather.2

commit v3 on v1

v3 whole, which is shorter than its diff:
```python
import numpy as np
import jax
import jax.numpy as jnp
from jax import lax
from jax.experimental import pallas as pl
from jax.experimental.pallas import tpu as pltpu
from jax.sharding import Mesh, PartitionSpec as P

NEG_FILL = -1e30
COL = ("ylo", "z", "core")


def from_behind(array, axis, by):
    count = lax.axis_size(axis)
    pairs = [(i, i + by) for i in range(count) if 0 <= i + by < count]
    return lax.ppermute(array, axis, pairs)


def encode(full, weights):
    out = lax.conv_general_dilated(
        full[None],
        weights,
        window_strides=(2, 2),
        padding="VALID",
        dimension_numbers=("NHWC", "HWIO", "NHWC"),
        preferred_element_type=jnp.float32,
    )
    return out[0].astype(jnp.bfloat16)


def corr_kernel(par_ref, q_ref, k_ref, peak_ref, mass_ref, mom_ref, spr_ref, *, blk, masked_steps):
    qg0 = par_ref[0]
    kofs = par_ref[1]
    n_plain = par_ref[2]
    mstart = par_ref[3]
    width = q_ref.shape[1]
    q = q_ref[0]
    scale = q.shape[-1] ** (-0.5)
    lane = lax.broadcasted_iota(jnp.int32, (1, width), 1).astype(jnp.float32)
    qpos = (qg0 * blk).astype(jnp.float32) + lane
    jcol = lax.broadcasted_iota(jnp.int32, (blk, 1), 0).astype(jnp.float32)

    def step(kb, state, masked):
        peak, mass, moment, spread = state
        start = pl.multiple_of(kb * blk, blk)
        keys = k_ref[0, pl.ds(start, blk), :]
        scores = lax.dot_general(
            keys, q, (((1,), (1,)), ((), ())), preferred_element_type=jnp.float32
        ) * scale
        base = qpos - ((kb + kofs) * blk).astype(jnp.float32)
        if masked:
            allowed = (base - jcol) >= 0.0
            scores = jnp.where(allowed, scores, NEG_FILL)
        new_peak = jnp.maximum(peak, jnp.max(scores, axis=0, keepdims=True))
        shifted = scores - new_peak
        if masked:
            shifted = jnp.where(allowed, shifted, NEG_FILL)
        weights = jnp.exp(shifted)
        settled = jnp.where(allowed, shifted, 0.0) if masked else shifted
        factor = jnp.exp(peak - new_peak)
        total = jnp.sum(weights, axis=0, keepdims=True)
        mass_new = mass * factor + total
        moment_new = moment * factor + (
            base * total - jnp.sum(weights * jcol, axis=0, keepdims=True)
        )
        spread_new = factor * (spread + (peak - new_peak) * mass) + jnp.sum(
            weights * settled, axis=0, keepdims=True
        )
        return (new_peak, mass_new, moment_new, spread_new)

    zeros = jnp.zeros((1, width), jnp.float32)
    state = (jnp.full((1, width), NEG_FILL, jnp.float32), zeros, zeros, zeros)
    state = lax.fori_loop(0, n_plain, lambda kb, s: step(kb, s, False), state)
    for extra in range(masked_steps):
        state = step(mstart + extra, state, True)
    for ref, value in zip((peak_ref, mass_ref, mom_ref, spr_ref), state):
        ref[0] = value


def correlate(params, queries, keys, blk, masked_steps):
    rows, width, feat = queries.shape
    total_cols = keys.shape[1]
    kernel = lambda *refs: corr_kernel(*refs, blk=blk, masked_steps=masked_steps)
    out_shape = jax.ShapeDtypeStruct((rows, 1, width), jnp.float32)
    out_spec = pl.BlockSpec((1, 1, width), lambda r, s: (r, 0, 0))
    state = pl.pallas_call(
        kernel,
        out_shape=(out_shape,) * 4,
        grid_spec=pltpu.PrefetchScalarGridSpec(
            num_scalar_prefetch=1,
            grid=(rows,),
            in_specs=[
                pl.BlockSpec((1, width, feat), lambda r, s: (r, 0, 0)),
                pl.BlockSpec((1, total_cols, feat), lambda r, s: (r, 0, 0)),
            ],
            out_specs=[out_spec] * 4,
        ),
        compiler_params=pltpu.CompilerParams(dimension_semantics=("arbitrary",)),
    )(params, queries, keys)
    return tuple(x.reshape(rows, width) for x in state)


def merge(one, two):
    p1, m1, mo1, s1 = one
    p2, m2, mo2, s2 = two
    peak = jnp.maximum(p1, p2)
    f1 = jnp.exp(p1 - peak)
    f2 = jnp.exp(p2 - peak)
    mass = m1 * f1 + m2 * f2
    moment = mo1 * f1 + mo2 * f2
    spread = f1 * (s1 + (p1 - peak) * m1) + f2 * (s2 + (p2 - peak) * m2)
    return (peak, mass, moment, spread)


def local(left_image, right_image, conv_weight):
    col_count = left_image.shape[1] // 2
    border = jnp.stack([left_image[:, -1:, :], right_image[:, -1:, :]])
    border = from_behind(border, COL, 1)
    left_wide = jnp.concatenate([border[0], left_image], axis=1)
    right_wide = jnp.concatenate([border[1], right_image], axis=1)
    upper = from_behind(jnp.stack([left_wide[-1:], right_wide[-1:]]), "row", 1)
    left_full = jnp.concatenate([upper[0], left_wide], axis=0)
    right_full = jnp.concatenate([upper[1], right_wide], axis=0)
    right_feat = encode(right_full, conv_weight)
    right_half = lax.all_to_all(right_feat, "core", 0, 1, tiled=True)
    keys = lax.all_gather(right_half, "z", axis=1, tiled=True)
    left_feat = encode(left_full, conv_weight)
    queries = lax.all_to_all(left_feat, "core", 0, 1, tiled=True)
    visiting = lax.ppermute(queries, "ylo", [(1, 0)])

    plane = lax.axis_index("ylo")
    zpos = lax.axis_index("z")
    per_chip = queries.shape[1] // col_count
    plane_blocks = keys.shape[1] // col_count
    kofs = plane * plane_blocks
    own_params = jnp.stack(
        [kofs + per_chip * zpos, kofs, per_chip * zpos, per_chip * zpos]
    ).astype(jnp.int32)
    own = correlate(own_params, queries, keys, col_count, per_chip)
    lower = (plane == 0).astype(jnp.int32)
    visit_params = jnp.stack(
        [plane_blocks + per_chip * zpos, jnp.int32(0), plane_blocks * lower, jnp.int32(0)]
    ).astype(jnp.int32)
    cross = correlate(visit_params, visiting, keys, col_count, 0)
    back = lax.ppermute(jnp.stack(cross), "ylo", [(0, 1)])
    merged = merge(own, tuple(back[i] for i in range(4)))
    upper_plane = plane == 1
    peak, mass, moment, spread = (
        jnp.where(upper_plane, m, o) for m, o in zip(merged, own)
    )
    disp = moment / mass / col_count
    ent = jnp.log(mass) - spread / mass
    both = lax.all_to_all(jnp.stack([disp, ent]), "core", 2, 1, tiled=True)
    return both[0], both[1]


def solution(mesh):
    rows, cols = mesh.devices.shape
    split = Mesh(
        np.asarray(mesh.devices).reshape(rows, 2, cols // 4, 2), ("row", "ylo", "z", "core")
    )
    in_specs = (P("row", COL, None), P("row", COL, None), P())
    out_specs = (P("row", COL), P("row", COL))
    return jax.shard_map(local, mesh=split, in_specs=in_specs, out_specs=out_specs, check_vma=False)
```

time: 190 us -> 150 us (0.79)
  the two profiles are of different devices: /device:TPU:233 before, /device:TPU:225 now
where the time goes in v3:
time: 150 us
  waiting for transfers between devices  46.2 us (31%)
  Pallas kernels  36.4 us (24%)
  matrix products  16.8 us (11%)
  blocking collectives  15.4 us (10%)
  between operations  14.2 us (9%)
  starting transfers between devices  7.85 us (5%)
  local copies, waits for them, and re-layouts  7.16 us (5%)
  other arithmetic  5.88 us (4%)
    pallas_call x2, Pallas kernels, correlate(): pl.pallas_call(kernel, out_shape=(out_shape,) * 4, grid_spec=pltpu.Prefet...  36.4 us
    all_gather x1, waiting for transfers between devices, local(): keys = lax.all_gather(right_half, 'z', axis=1, tiled=True)  28.3 us
    conv_general_dilated x2, matrix products, encode(): lax.conv_general_dilated(full[None], weights, window_strides=(2, 2), padd...  16.8 us
    ppermute x1, waiting for transfers between devices, local(): visiting = lax.ppermute(queries, 'ylo', [(1, 0)])  13.2 us
    all_to_all x1, blocking collectives, local(): right_half = lax.all_to_all(right_feat, 'core', 0, 1, tiled=True)  7.16 us
    ppermute x2, starting transfers between devices, from_behind(): return lax.ppermute(array, axis, pairs)  5.05 us
    ppermute x2, waiting for transfers between devices, from_behind(): return lax.ppermute(array, axis, pairs)  4.64 us
    all_to_all x1, blocking collectives, local(): queries = lax.all_to_all(left_feat, 'core', 0, 1, tiled=True)  4.15 us
  transfers between devices with their start and end apart: 5, of which 4 were waited for; matrix products, arithmetic and copies ran while one was open for 7% of the time, Pallas kernels for 12%

profile of v3, /device:TPU:225, one launch (start us, length us, event | category | flops | bytes accessed | tf_op | source)
XLA Modules:
  0.0 150.0 jit_solution(6203602946118117862)
XLA Ops:
  7.2 0.0 copy-start
  7.2 0.0 copy-start.1
  7.2 0.0 all-gather.2.cloned.1.call-start
  7.2 0.8 slice.44
  8.1 0.7 slice.45
  8.8 1.9 %collective-permute-start = (bf16[2,8,1,128]{3,1,2,0:T(8,128)(2,1)S(1)}, bf16[2,8,1,128]{3,1,2,0:T(8,128)(2,1)S(1)}, u32[]{:S(2)}, u32[]{:S(2)}) collective-permute-start(bf16[2,8,1,128]{3,1,2,0:T(8,128)(2,1)S(1)} %pad_maximum_fusion.5), channel_id=1, source_target_pairs={{0,1},{1,2},{2,3},{3,4},{4,5},{5,6},{6,7},{7,8},{8,9},{9,10},{10,1... | collective-permute-start | bytes 12296 | tf_op jit(solution)/shard_map/ppermute | solution.py:16
  10.7 1.3 collective-permute-done
  12.1 0.9 fusion.10
  13.0 0.9 fusion.11
  14.0 3.1 %collective-permute-start.1 = (bf16[2,1,513,128]{3,2,1,0:T(8,128)(2,1)S(1)}, bf16[2,1,513,128]{3,2,1,0:T(8,128)(2,1)S(1)}, u32[]{:S(2)}, u32[]{:S(2)}) collective-permute-start(bf16[2,1,513,128]{3,2,1,0:T(8,128)(2,1)S(1)} %pad_maximum_fusion), channel_id=1, source_target_pairs={{0,32},{32,64},{64,96},{96,128},{128,160},{160,192},{192,224},{1,3... | collective-permute-start | bytes 787976 | tf_op jit(solution)/shard_map/ppermute | solution.py:16
  17.1 3.3 %collective-permute-done.1 = bf16[2,1,513,128]{3,2,1,0:T(8,128)(2,1)S(1)} collective-permute-done((bf16[2,1,513,128]{3,2,1,0:T(8,128)(2,1)S(1)}, bf16[2,1,513,128]{3,2,1,0:T(8,128)(2,1)S(1)}, u32[]{:S(2)}, u32[]{:S(2)}) %collective-permute-start.1) | collective-permute-done | bytes 262688 | tf_op jit(solution)/shard_map/ppermute | solution.py:16
  20.5 0.0 copy-done.1
  20.5 0.3 maximum_bitcast_fusion.1
  20.8 0.0 copy-done
  20.8 8.4 %fusion.7 = bf16[1,4,256,256]{3,0,2,1:T(2,128)(2,1)S(1)} fusion(bf16[3,3,128,256]{3,2,1,0:T(8,128)(2,1)S(1)} %copy-done, bf16[1,9,513,128]{3,2,1,0:T(8,128)(2,1)S(1)} %maximum_bitcast_fusion.1), kind=kOutput, calls=%fused_computation.5 | convolution fusion | flops 604241920 | bytes 2296064 | tf_op jit(solution)/shard_map/conv_general_dilated | solution.py:20
  29.2 0.0 copy-start.2
  29.3 0.1 copy.58
  29.4 7.2 %all_to_all.51 = bf16[4,256,256]{2,1,0:T(8,128)(2,1)S(1)} all-to-all(bf16[4,256,256]{2,1,0:T(8,128)(2,1)S(1)} %bitcast.96), channel_id=1, replica_groups=mesh['row'=8,'ylo'=2,'z'=8,'core'=2] {'core'}, dimensions={0} | all-to-all | bytes 1048576 | tf_op jit(solution)/shard_map/all_to_all | solution.py:125
  36.5 0.8 copy.38
  37.4 0.0 all-gather.2.cloned.1.call-update
  37.4 0.3 maximum_bitcast_fusion
  37.7 8.4 %fusion.4 = bf16[1,4,256,256]{3,0,2,1:T(2,128)(2,1)S(1)} fusion(bf16[3,3,128,256]{3,2,1,0:T(8,128)(2,1)S(1)} %copy-done, bf16[1,9,513,128]{3,2,1,0:T(8,128)(2,1)S(1)} %maximum_bitcast_fusion), kind=kOutput, calls=%fused_computation.4 | convolution fusion | flops 604241920 | bytes 2296064 | tf_op jit(solution)/shard_map/conv_general_dilated | solution.py:20
  46.1 0.1 copy.59
  46.2 4.2 %all_to_all.52 = bf16[4,256,256]{2,1,0:T(8,128)(2,1)S(1)} all-to-all(bf16[4,256,256]{2,1,0:T(8,128)(2,1)S(1)} %bitcast.97), channel_id=1, replica_groups=mesh['row'=8,'ylo'=2,'z'=8,'core'=2] {'core'}, dimensions={0} | all-to-all | bytes 1048576 | tf_op jit(solution)/shard_map/all_to_all | solution.py:128
  50.4 1.3 collective-permute-start.2
  51.7 0.6 pad_add_fusion.1.refs_0_
  52.3 13.2 %collective-permute-done.2.refs_1_ = bf16[2,512,256]{2,1,0:T(8,128)(2,1)S(1)} collective-permute-done((bf16[2,512,256]{2,1,0:T(8,128)(2,1)S(1)}, bf16[2,512,256]{2,1,0:T(8,128)(2,1)S(1)}, u32[]{:S(2)}, u32[]{:S(2)}) %collective-permute-start.2) | collective-permute-done | bytes 524320 | tf_op jit(solution)/shard_map/ppermute | solution.py:129
  65.6 28.3 %all-gather.2.cloned.1.call-done.refs_2_ = bf16[2,4096,256]{2,1,0:T(8,128)(2,1)} async-done(((bf16[2,512,256]{2,1,0:T(8,128)(2,1)}), bf16[2,4096,256]{2,1,0:T(8,128)(2,1)}) %all-gather.2.cloned.1.call-update) | async-done | bytes 4194320 | tf_op jit(solution)/shard_map/all_gather | solution.py:126
  93.9 0.0 copy-done.4
  93.9 18.3 %shard_map.51 = (f32[2,1,512]{2,1,0:T(1,128)}, f32[2,1,512]{2,1,0:T(1,128)}, f32[2,1,512]{2,1,0:T(1,128)}, f32[2,1,512]{2,1,0:T(1,128)}) custom-call(s32[4]{0:T(128)} %pad_add_fusion.1.refs_0_, bf16[2,512,256]{2,1,0:T(8,128)(2,1)} %copy-done.4, bf16[2,4096,256]{2,1,0:T(8,128)(2,1)} %all-gather.2.cloned.1.call-done.refs_2_), custom_call_target="tpu_custom_call" | custom-call | tf_op jit(solution)/shard_map/pallas_call | solution.py:86
  112.2 0.0 copy-done.3
  112.2 0.7 pad_maximum_fusion.3
  113.0 1.5 collective-permute-start.3
  114.4 0.6 pad_add_fusion.refs_0_
  115.0 18.1 %shard_map.50 = (f32[2,1,512]{2,1,0:T(1,128)}, f32[2,1,512]{2,1,0:T(1,128)}, f32[2,1,512]{2,1,0:T(1,128)}, f32[2,1,512]{2,1,0:T(1,128)}) custom-call(s32[4]{0:T(128)} %pad_add_fusion.refs_0_, bf16[2,512,256]{2,1,0:T(8,128)(2,1)} %bitcast.95, bf16[2,4096,256]{2,1,0:T(8,128)(2,1)} %all-gather.2.cloned.1.call-done.refs_2_), custom_call_target="tpu_custom_call" | custom-call | tf_op jit(solution)/shard_map/pallas_call | solution.py:86
  133.1 0.0 collective-permute-done.3
  133.1 0.8 fusion.19
  133.9 0.3 copy.39
  134.2 0.7 reshape.32
  134.9 4.0 %all_to_all.53 = f32[2,1,1024]{2,1,0:T(1,128)S(1)} all-to-all(f32[2,1,1024]{2,1,0:T(1,128)S(1)} %reshape.32), channel_id=1, replica_groups=mesh['row'=8,'ylo'=2,'z'=8,'core'=2] {'core'}, dimensions={0} | all-to-all | bytes 16384 | tf_op jit(solution)/shard_map/all_to_all | solution.py:153
  138.9 0.5 broadcast.7
  139.4 0.7 reduce
  140.1 0.8 reshape.33
  140.9 0.6 fusion.20
  141.5 0.2 copy.40
  141.7 0.6 squeeze.28
  142.3 0.2 copy.41
  142.5 0.6 squeeze.29
  (12 shorter events, 0.1 us)
Async XLA Ops:
  7.2 13.6 %copy-start = (bf16[3,3,128,256]{3,2,1,0:T(8,128)(2,1)S(1)}, bf16[3,3,128,256]{3,2,1,0:T(8,128)(2,1)}, u32[]{:S(2)}) copy-start(bf16[3,3,128,256]{3,2,1,0:T(8,128)(2,1)} %param.5) | copy-start | bytes 1769476
  7.2 13.3 %copy-start.1 = (bf16[8,512,128]{2,1,0:T(8,128)(2,1)S(1)}, bf16[8,512,128]{2,1,0:T(8,128)(2,1)}, u32[]{:S(2)}) copy-start(bf16[8,512,128]{2,1,0:T(8,128)(2,1)} %param.4) | copy-start | bytes 3145732
  7.2 86.7 %all-gather.2.cloned.1.call-start = ((), (), s32[]{:S(2)}) async-start(), calls=%async_computation.3 | async-start | bytes 4718592 | tf_op jit(solution)/shard_map/all_gather | solution.py:126
  8.8 3.2 %collective-permute-start = (bf16[2,8,1,128]{3,1,2,0:T(8,128)(2,1)S(1)}, bf16[2,8,1,128]{3,1,2,0:T(8,128)(2,1)S(1)}, u32[]{:S(2)}, u32[]{:S(2)}) collective-permute-start(bf16[2,8,1,128]{3,1,2,0:T(8,128)(2,1)S(1)} %pad_maximum_fusion.5), channel_id=1, source_target_pairs={{0,1},{1,2},{2,3},{3,4},{4,5},{5,6},{6,7},{7,8},{8,9},{9,10},{10,1... | collective-permute-start | bytes 12296 | tf_op jit(solution)/shard_map/ppermute | solution.py:16
  14.0 6.5 %collective-permute-start.1 = (bf16[2,1,513,128]{3,2,1,0:T(8,128)(2,1)S(1)}, bf16[2,1,513,128]{3,2,1,0:T(8,128)(2,1)S(1)}, u32[]{:S(2)}, u32[]{:S(2)}) collective-permute-start(bf16[2,1,513,128]{3,2,1,0:T(8,128)(2,1)S(1)} %pad_maximum_fusion), channel_id=1, source_target_pairs={{0,32},{32,64},{64,96},{96,128},{128,160},{160,192},{192,224},{1,3... | collective-permute-start | bytes 787976 | tf_op jit(solution)/shard_map/ppermute | solution.py:16
  29.2 8.1 %copy-start.2 = (bf16[8,512,128]{2,1,0:T(8,128)(2,1)S(1)}, bf16[8,512,128]{2,1,0:T(8,128)(2,1)}, u32[]{:S(2)}) copy-start(bf16[8,512,128]{2,1,0:T(8,128)(2,1)} %param.3) | copy-start | bytes 3145732
  50.4 61.8 %copy-start.3 = (bf16[2,2,256,256]{3,2,0,1:T(8,128)(2,1)}, bf16[2,2,256,256]{3,2,0,1:T(8,128)(2,1)S(1)}, u32[]{:S(2)}) copy-start(bf16[2,2,256,256]{3,2,0,1:T(8,128)(2,1)S(1)} %copy.36) | copy-start | bytes 1572868
  50.4 15.1 %collective-permute-start.2 = (bf16[2,512,256]{2,1,0:T(8,128)(2,1)S(1)}, bf16[2,512,256]{2,1,0:T(8,128)(2,1)S(1)}, u32[]{:S(2)}, u32[]{:S(2)}) collective-permute-start(bf16[2,512,256]{2,1,0:T(8,128)(2,1)S(1)} %bitcast.94), channel_id=1, source_target_pairs={{16,0},{17,1},{18,2},{19,3},{20,4},{21,5},{22,6},{23,7},{24,8},{25... | collective-permute-start | bytes 1572872 | tf_op jit(solution)/shard_map/ppermute | solution.py:129
  65.5 28.3 %copy-start.4 = (bf16[2,512,256]{2,1,0:T(8,128)(2,1)}, bf16[2,512,256]{2,1,0:T(8,128)(2,1)S(1)}, u32[]{:S(2)}) copy-start(bf16[2,512,256]{2,1,0:T(8,128)(2,1)S(1)} %collective-permute-done.2.refs_1_) | copy-start | bytes 1572868
  113.0 20.2 %collective-permute-start.3 = (f32[4,2,512]{2,0,1:T(4,128)S(1)}, f32[4,2,512]{2,0,1:T(4,128)S(1)}, u32[]{:S(2)}, u32[]{:S(2)}) collective-permute-start(f32[4,2,512]{2,0,1:T(4,128)S(1)} %pad_maximum_fusion.3), channel_id=1, source_target_pairs={{0,16},{1,17},{2,18},{3,19},{4,20},{5,21},{6,22},{7,23},{8,24},{9,... | collective-permute-start | bytes 49160 | tf_op jit(solution)/shard_map/ppermute | solution.py:145
Sparse Core Ops, SparseCore 0:
  37.5 56.3 all-gather.1

commit v4 on v3

--- a/solution.py
+++ b/solution.py
@@ -28,7 +28,7 @@
     return out[0].astype(jnp.bfloat16)
 
 
-def corr_kernel(par_ref, q_ref, k_ref, peak_ref, mass_ref, mom_ref, spr_ref, *, blk, masked_steps):
+def corr_kernel(par_ref, q_ref, k_ref, peak_ref, mass_ref, mom_ref, spr_ref, s_ref, *, blk, masked_steps):
     qg0 = par_ref[0]
     kofs = par_ref[1]
     n_plain = par_ref[2]
@@ -68,9 +68,45 @@
         )
         return (new_peak, mass_new, moment_new, spread_new)
 
+    sub = 8
+    rsub = lax.broadcasted_iota(jnp.int32, (sub, 1), 0).astype(jnp.float32)
+
+    def plain_step(kb, state):
+        peak, mass, moment, spread = state
+        start = pl.multiple_of(kb * blk, blk)
+        keys = k_ref[0, pl.ds(start, blk), :]
+        s_ref[...] = lax.dot_general(
+            keys, q, (((1,), (1,)), ((), ())), preferred_element_type=jnp.float32
+        )
+        base = qpos - ((kb + kofs) * blk).astype(jnp.float32)
+        new_peak = jnp.maximum(peak, jnp.max(s_ref[...], axis=0, keepdims=True) * scale)
+
+        def chunk(i, accs):
+            acc_w, acc_iw, acc_wt = accs
+            row = pl.multiple_of(i * sub, sub)
+            shifted = s_ref[pl.ds(row, sub), :] * scale - new_peak
+            weights = jnp.exp(shifted)
+            return (
+                acc_w + weights,
+                acc_iw + weights * i.astype(jnp.float32),
+                acc_wt + weights * shifted,
+            )
+
+        zero = jnp.zeros((sub, width), jnp.float32)
+        acc_w, acc_iw, acc_wt = lax.fori_loop(0, blk // sub, chunk, (zero, zero, zero), unroll=8)
+        total = jnp.sum(acc_w, axis=0, keepdims=True)
+        weighted_j = jnp.sum(acc_iw * float(sub) + acc_w * rsub, axis=0, keepdims=True)
+        factor = jnp.exp(peak - new_peak)
+        mass_new = mass * factor + total
+        moment_new = moment * factor + (base * total - weighted_j)
+        spread_new = factor * (spread + (peak - new_peak) * mass) + jnp.sum(
+            acc_wt, axis=0, keepdims=True
+        )
+        return (new_peak, mass_new, moment_new, spread_new)
+
     zeros = jnp.zeros((1, width), jnp.float32)
     state = (jnp.full((1, width), NEG_FILL, jnp.float32), zeros, zeros, zeros)
-    state = lax.fori_loop(0, n_plain, lambda kb, s: step(kb, s, False), state)
+    state = lax.fori_loop(0, n_plain, plain_step, state)
     for extra in range(masked_steps):
         state = step(mstart + extra, state, True)
     for ref, value in zip((peak_ref, mass_ref, mom_ref, spr_ref), state):
@@ -94,6 +130,7 @@
                 pl.BlockSpec((1, total_cols, feat), lambda r, s: (r, 0, 0)),
             ],
             out_specs=[out_spec] * 4,
+            scratch_shapes=[pltpu.VMEM((blk, width), jnp.float32)],
         ),
         compiler_params=pltpu.CompilerParams(dimension_semantics=("arbitrary",)),
     )(params, queries, keys)

time: 150 us -> 150 us (level)
  no operation moved by 1% of the time
where the time goes in v4:
time: 150 us
  waiting for transfers between devices  46.2 us (31%)
  Pallas kernels  36.4 us (24%)
  matrix products  16.8 us (11%)
  blocking collectives  15.4 us (10%)
  between operations  14.2 us (9%)
  starting transfers between devices  7.85 us (5%)
  local copies, waits for them, and re-layouts  7.16 us (5%)
  other arithmetic  5.88 us (4%)
    pallas_call x2, Pallas kernels, correlate(): pl.pallas_call(kernel, out_shape=(out_shape,) * 4, grid_spec=pltpu.Prefet...  36.4 us
    all_gather x1, waiting for transfers between devices, local(): keys = lax.all_gather(right_half, 'z', axis=1, tiled=True)  28.3 us
    conv_general_dilated x2, matrix products, encode(): lax.conv_general_dilated(full[None], weights, window_strides=(2, 2), padd...  16.8 us
    ppermute x1, waiting for transfers between devices, local(): visiting = lax.ppermute(queries, 'ylo', [(1, 0)])  13.2 us
    all_to_all x1, blocking collectives, local(): right_half = lax.all_to_all(right_feat, 'core', 0, 1, tiled=True)  7.16 us
    ppermute x2, starting transfers between devices, from_behind(): return lax.ppermute(array, axis, pairs)  5.05 us
    ppermute x2, waiting for transfers between devices, from_behind(): return lax.ppermute(array, axis, pairs)  4.64 us
    all_to_all x1, blocking collectives, local(): queries = lax.all_to_all(left_feat, 'core', 0, 1, tiled=True)  4.15 us
  transfers between devices with their start and end apart: 5, of which 4 were waited for; matrix products, arithmetic and copies ran while one was open for 7% of the time, Pallas kernels for 12%

profile of v4, /device:TPU:225, one launch (start us, length us, event | category | flops | bytes accessed | tf_op | source)
XLA Modules:
  0.0 150.0 jit_solution(5462077701373303259)
XLA Ops:
  7.2 0.0 copy-start
  7.2 0.0 copy-start.1
  7.2 0.0 all-gather.2.cloned.1.call-start
  7.2 0.8 slice.44
  8.1 0.7 slice.45
  8.8 1.9 %collective-permute-start = (bf16[2,8,1,128]{3,1,2,0:T(8,128)(2,1)S(1)}, bf16[2,8,1,128]{3,1,2,0:T(8,128)(2,1)S(1)}, u32[]{:S(2)}, u32[]{:S(2)}) collective-permute-start(bf16[2,8,1,128]{3,1,2,0:T(8,128)(2,1)S(1)} %pad_maximum_fusion.5), channel_id=1, source_target_pairs={{0,1},{1,2},{2,3},{3,4},{4,5},{5,6},{6,7},{7,8},{8,9},{9,10},{10,1... | collective-permute-start | bytes 12296 | tf_op jit(solution)/shard_map/ppermute | solution.py:16
  10.7 1.3 collective-permute-done
  12.1 0.9 fusion.10
  13.0 0.9 fusion.11
  14.0 3.1 %collective-permute-start.1 = (bf16[2,1,513,128]{3,2,1,0:T(8,128)(2,1)S(1)}, bf16[2,1,513,128]{3,2,1,0:T(8,128)(2,1)S(1)}, u32[]{:S(2)}, u32[]{:S(2)}) collective-permute-start(bf16[2,1,513,128]{3,2,1,0:T(8,128)(2,1)S(1)} %pad_maximum_fusion), channel_id=1, source_target_pairs={{0,32},{32,64},{64,96},{96,128},{128,160},{160,192},{192,224},{1,3... | collective-permute-start | bytes 787976 | tf_op jit(solution)/shard_map/ppermute | solution.py:16
  17.1 3.3 %collective-permute-done.1 = bf16[2,1,513,128]{3,2,1,0:T(8,128)(2,1)S(1)} collective-permute-done((bf16[2,1,513,128]{3,2,1,0:T(8,128)(2,1)S(1)}, bf16[2,1,513,128]{3,2,1,0:T(8,128)(2,1)S(1)}, u32[]{:S(2)}, u32[]{:S(2)}) %collective-permute-start.1) | collective-permute-done | bytes 262688 | tf_op jit(solution)/shard_map/ppermute | solution.py:16
  20.5 0.0 copy-done.1
  20.5 0.3 maximum_bitcast_fusion.1
  20.8 0.0 copy-done
  20.8 8.4 %fusion.7 = bf16[1,4,256,256]{3,0,2,1:T(2,128)(2,1)S(1)} fusion(bf16[3,3,128,256]{3,2,1,0:T(8,128)(2,1)S(1)} %copy-done, bf16[1,9,513,128]{3,2,1,0:T(8,128)(2,1)S(1)} %maximum_bitcast_fusion.1), kind=kOutput, calls=%fused_computation.5 | convolution fusion | flops 604241920 | bytes 2296064 | tf_op jit(solution)/shard_map/conv_general_dilated | solution.py:20
  29.2 0.0 copy-start.2
  29.3 0.1 copy.58
  29.4 7.2 %all_to_all.51 = bf16[4,256,256]{2,1,0:T(8,128)(2,1)S(1)} all-to-all(bf16[4,256,256]{2,1,0:T(8,128)(2,1)S(1)} %bitcast.96), channel_id=1, replica_groups=mesh['row'=8,'ylo'=2,'z'=8,'core'=2] {'core'}, dimensions={0} | all-to-all | bytes 1048576 | tf_op jit(solution)/shard_map/all_to_all | solution.py:162
  36.5 0.8 copy.38
  37.4 0.0 all-gather.2.cloned.1.call-update
  37.4 0.0 copy-done.2
  37.4 0.3 maximum_bitcast_fusion
  37.7 8.4 %fusion.4 = bf16[1,4,256,256]{3,0,2,1:T(2,128)(2,1)S(1)} fusion(bf16[3,3,128,256]{3,2,1,0:T(8,128)(2,1)S(1)} %copy-done, bf16[1,9,513,128]{3,2,1,0:T(8,128)(2,1)S(1)} %maximum_bitcast_fusion), kind=kOutput, calls=%fused_computation.4 | convolution fusion | flops 604241920 | bytes 2296064 | tf_op jit(solution)/shard_map/conv_general_dilated | solution.py:20
  46.1 0.1 copy.59
  46.2 4.2 %all_to_all.52 = bf16[4,256,256]{2,1,0:T(8,128)(2,1)S(1)} all-to-all(bf16[4,256,256]{2,1,0:T(8,128)(2,1)S(1)} %bitcast.97), channel_id=1, replica_groups=mesh['row'=8,'ylo'=2,'z'=8,'core'=2] {'core'}, dimensions={0} | all-to-all | bytes 1048576 | tf_op jit(solution)/shard_map/all_to_all | solution.py:165
  50.4 1.3 collective-permute-start.2
  51.7 0.6 pad_add_fusion.1.refs_0_
  52.3 13.2 %collective-permute-done.2.refs_1_ = bf16[2,512,256]{2,1,0:T(8,128)(2,1)S(1)} collective-permute-done((bf16[2,512,256]{2,1,0:T(8,128)(2,1)S(1)}, bf16[2,512,256]{2,1,0:T(8,128)(2,1)S(1)}, u32[]{:S(2)}, u32[]{:S(2)}) %collective-permute-start.2) | collective-permute-done | bytes 524320 | tf_op jit(solution)/shard_map/ppermute | solution.py:166
  65.6 28.3 %all-gather.2.cloned.1.call-done.refs_2_ = bf16[2,4096,256]{2,1,0:T(8,128)(2,1)} async-done(((bf16[2,512,256]{2,1,0:T(8,128)(2,1)}), bf16[2,4096,256]{2,1,0:T(8,128)(2,1)}) %all-gather.2.cloned.1.call-update) | async-done | bytes 4194320 | tf_op jit(solution)/shard_map/all_gather | solution.py:163
  93.9 0.0 copy-done.4
  93.9 18.3 %shard_map.51 = (f32[2,1,512]{2,1,0:T(1,128)}, f32[2,1,512]{2,1,0:T(1,128)}, f32[2,1,512]{2,1,0:T(1,128)}, f32[2,1,512]{2,1,0:T(1,128)}) custom-call(s32[4]{0:T(128)} %pad_add_fusion.1.refs_0_, bf16[2,512,256]{2,1,0:T(8,128)(2,1)} %copy-done.4, bf16[2,4096,256]{2,1,0:T(8,128)(2,1)} %all-gather.2.cloned.1.call-done.refs_2_), custom_call_target="tpu_custom_call" | custom-call | tf_op jit(solution)/shard_map/pallas_call | solution.py:122
  112.2 0.7 pad_maximum_fusion.3
  112.9 1.5 collective-permute-start.3
  114.4 0.6 pad_add_fusion.refs_0_
  115.0 18.1 %shard_map.50 = (f32[2,1,512]{2,1,0:T(1,128)}, f32[2,1,512]{2,1,0:T(1,128)}, f32[2,1,512]{2,1,0:T(1,128)}, f32[2,1,512]{2,1,0:T(1,128)}) custom-call(s32[4]{0:T(128)} %pad_add_fusion.refs_0_, bf16[2,512,256]{2,1,0:T(8,128)(2,1)} %bitcast.95, bf16[2,4096,256]{2,1,0:T(8,128)(2,1)} %all-gather.2.cloned.1.call-done.refs_2_), custom_call_target="tpu_custom_call" | custom-call | tf_op jit(solution)/shard_map/pallas_call | solution.py:122
  133.1 0.0 collective-permute-done.3
  133.1 0.8 fusion.19
  133.9 0.3 copy.39
  134.2 0.7 reshape.32
  134.8 4.0 %all_to_all.53 = f32[2,1,1024]{2,1,0:T(1,128)S(1)} all-to-all(f32[2,1,1024]{2,1,0:T(1,128)S(1)} %reshape.32), channel_id=1, replica_groups=mesh['row'=8,'ylo'=2,'z'=8,'core'=2] {'core'}, dimensions={0} | all-to-all | bytes 16384 | tf_op jit(solution)/shard_map/all_to_all | solution.py:190
  138.9 0.5 broadcast.7
  139.4 0.7 reduce
  140.1 0.8 reshape.33
  140.9 0.6 fusion.20
  141.5 0.2 copy.40
  141.7 0.6 squeeze.28
  142.3 0.2 copy.41
  142.5 0.6 squeeze.29
  (12 shorter events, 0.1 us)
Async XLA Ops:
  7.2 13.6 %copy-start = (bf16[3,3,128,256]{3,2,1,0:T(8,128)(2,1)S(1)}, bf16[3,3,128,256]{3,2,1,0:T(8,128)(2,1)}, u32[]{:S(2)}) copy-start(bf16[3,3,128,256]{3,2,1,0:T(8,128)(2,1)} %param.5) | copy-start | bytes 1769476
  7.2 13.3 %copy-start.1 = (bf16[8,512,128]{2,1,0:T(8,128)(2,1)S(1)}, bf16[8,512,128]{2,1,0:T(8,128)(2,1)}, u32[]{:S(2)}) copy-start(bf16[8,512,128]{2,1,0:T(8,128)(2,1)} %param.4) | copy-start | bytes 3145732
  7.2 86.7 %all-gather.2.cloned.1.call-start = ((), (), s32[]{:S(2)}) async-start(), calls=%async_computation.3 | async-start | bytes 4718592 | tf_op jit(solution)/shard_map/all_gather | solution.py:163
  8.8 3.2 %collective-permute-start = (bf16[2,8,1,128]{3,1,2,0:T(8,128)(2,1)S(1)}, bf16[2,8,1,128]{3,1,2,0:T(8,128)(2,1)S(1)}, u32[]{:S(2)}, u32[]{:S(2)}) collective-permute-start(bf16[2,8,1,128]{3,1,2,0:T(8,128)(2,1)S(1)} %pad_maximum_fusion.5), channel_id=1, source_target_pairs={{0,1},{1,2},{2,3},{3,4},{4,5},{5,6},{6,7},{7,8},{8,9},{9,10},{10,1... | collective-permute-start | bytes 12296 | tf_op jit(solution)/shard_map/ppermute | solution.py:16
  14.0 6.5 %collective-permute-start.1 = (bf16[2,1,513,128]{3,2,1,0:T(8,128)(2,1)S(1)}, bf16[2,1,513,128]{3,2,1,0:T(8,128)(2,1)S(1)}, u32[]{:S(2)}, u32[]{:S(2)}) collective-permute-start(bf16[2,1,513,128]{3,2,1,0:T(8,128)(2,1)S(1)} %pad_maximum_fusion), channel_id=1, source_target_pairs={{0,32},{32,64},{64,96},{96,128},{128,160},{160,192},{192,224},{1,3... | collective-permute-start | bytes 787976 | tf_op jit(solution)/shard_map/ppermute | solution.py:16
  29.2 8.1 %copy-start.2 = (bf16[8,512,128]{2,1,0:T(8,128)(2,1)S(1)}, bf16[8,512,128]{2,1,0:T(8,128)(2,1)}, u32[]{:S(2)}) copy-start(bf16[8,512,128]{2,1,0:T(8,128)(2,1)} %param.3) | copy-start | bytes 3145732
  50.4 61.8 %copy-start.3 = (bf16[2,2,256,256]{3,2,0,1:T(8,128)(2,1)}, bf16[2,2,256,256]{3,2,0,1:T(8,128)(2,1)S(1)}, u32[]{:S(2)}) copy-start(bf16[2,2,256,256]{3,2,0,1:T(8,128)(2,1)S(1)} %copy.36) | copy-start | bytes 1572868
  50.4 15.1 %collective-permute-start.2 = (bf16[2,512,256]{2,1,0:T(8,128)(2,1)S(1)}, bf16[2,512,256]{2,1,0:T(8,128)(2,1)S(1)}, u32[]{:S(2)}, u32[]{:S(2)}) collective-permute-start(bf16[2,512,256]{2,1,0:T(8,128)(2,1)S(1)} %bitcast.94), channel_id=1, source_target_pairs={{16,0},{17,1},{18,2},{19,3},{20,4},{21,5},{22,6},{23,7},{24,8},{25... | collective-permute-start | bytes 1572872 | tf_op jit(solution)/shard_map/ppermute | solution.py:166
  65.5 28.3 %copy-start.4 = (bf16[2,512,256]{2,1,0:T(8,128)(2,1)}, bf16[2,512,256]{2,1,0:T(8,128)(2,1)S(1)}, u32[]{:S(2)}) copy-start(bf16[2,512,256]{2,1,0:T(8,128)(2,1)S(1)} %collective-permute-done.2.refs_1_) | copy-start | bytes 1572868
  112.9 20.2 %collective-permute-start.3 = (f32[4,2,512]{2,0,1:T(4,128)S(1)}, f32[4,2,512]{2,0,1:T(4,128)S(1)}, u32[]{:S(2)}, u32[]{:S(2)}) collective-permute-start(f32[4,2,512]{2,0,1:T(4,128)S(1)} %pad_maximum_fusion.3), channel_id=1, source_target_pairs={{0,16},{1,17},{2,18},{3,19},{4,20},{5,21},{6,22},{7,23},{8,24},{9,... | collective-permute-start | bytes 49160 | tf_op jit(solution)/shard_map/ppermute | solution.py:182
Sparse Core Ops, SparseCore 0:
  37.5 56.3 all-gather.1
